TPU v7x, 128 devices: a whole 4x4x4 slice. The times are simulated.
128 devices in a mesh: img: 8 (over y, core), fsdp: 16 (over x, z).
Axes of the slice: x: 4, y: 4, z: 4, core: 2. Of those that a mesh axis runs over, the one named last changes fastest.
Arguments:
- text_states: bfloat16 [4096, 8192], P('img', 'fsdp'), may hold values from -100 to 100, as said below
- text_gain: float32 [8192], P('fsdp'), may hold values from 0.1 to 1.9
- gate_scale: float32 [8192], P('fsdp'), may hold values from 0.3 to 1.5
- live_counts: int32 [8], P('img'), may hold values from 1 to 512, 3072 in all
- token_slot: int32 [8, 512], P('img'), may hold values from 0 to 7, never falling along the last dimension, each value on 1 to 256 neighbouring positions
- wanted_images: int32 [8, 8], replicated, may hold values from 0 to 31, as said below
- patches: bfloat16 [32, 256, 1280], P('img', None, 'fsdp'), may hold values from -100 to 100, as said below
- latent_init: bfloat16 [64, 1280], replicated, may hold values from -100 to 100, as said below
- context_gain: float32 [1280], replicated, may hold values from 0.1 to 1.9
- latent_gain: float32 [1280], replicated, may hold values from 0.1 to 1.9
- res_query: bfloat16 [1280, 1536], P(None, 'fsdp'), may hold values from -0.15625 to 0.15625
- res_key: bfloat16 [1280, 1536], P(None, 'fsdp'), may hold values from -0.15625 to 0.15625
- res_value: bfloat16 [1280, 1536], P(None, 'fsdp'), may hold values from -0.15625 to 0.15625
- res_out: bfloat16 [1536, 1280], P('fsdp'), may hold values from -0.21875 to 0.21875
- final_gain: float32 [1280], P('fsdp'), may hold values from 0.1 to 1.9
- cross_query: bfloat16 [8192, 8192], P('fsdp'), may hold values from -0.09375 to 0.09375
- cross_key: bfloat16 [1280, 8192], P('fsdp'), may hold values from -0.25 to 0.25
- cross_value: bfloat16 [1280, 8192], P('fsdp'), may hold values from -0.25 to 0.25
- cross_out: bfloat16 [8192, 8192], P('fsdp'), may hold values from -0.09375 to 0.09375
Outputs:
- layer_output: float32 [4096, 8192], P('img', 'fsdp')
Inputs may be any that keep to these rules, and one draw needn't show every extreme that they name: `wanted_images`: image i is held by owner i // 4 along img. A row lists 8 distinct images; every owner that appears in a row has exactly 2 of its images there. `token_slot`: along a shard's tokens the slot never falls, and every slot of the shard is used. Tokens of shard s at positions live_counts[s] and beyond are padding. `text_states`: real values. `patches`: real values. `latent_init`: real values.
All inputs are finite; a program needn't handle non-finite values.
Results may differ from a plain program's by a relative error of at most 0.0075.
Values may be sent and summed in bfloat16 or wider, within the bound.
No kernel may reach another device: no remote copies, remote signals or barrier semaphores. Data moves between devices by JAX's collectives and lax.ppermute only.
A program may use at most 128 MiB of HBM per device.

v0:
```python
import jax
import jax.numpy as jnp
from jax import lax
from jax.sharding import PartitionSpec as P

D = 8192
HEAD = 128
RHD = 96
PAIR = 2
eps_norm = 1e-05
eps_rms = 1e-06


def layer_norm(values, gain_vec):
    values = values.astype(jnp.float32)
    row_mean = jnp.mean(values, -1, keepdims=True)
    spread = jnp.mean(values * values, -1, keepdims=True) - row_mean * row_mean
    return (values - row_mean) * lax.rsqrt(spread + eps_norm) * gain_vec


def route_tables(wanted_images, per_owner, pair_slots):
    owners = wanted_images // per_owner
    slot_total = wanted_images.shape[1]
    positions = jnp.arange(slot_total, dtype=jnp.int32)
    before = (owners[:, :, None] == owners[:, None, :]) & (
        positions[None, None, :] < positions[None, :, None]
    )
    slot_rank = jnp.sum(before.astype(jnp.int32), axis=2)
    rank_hot = (
        slot_rank[:, :, None] == jnp.arange(pair_slots, dtype=jnp.int32)[None, None, :]
    ).astype(jnp.float32)
    return (owners, rank_hot)


def pack_rows(row_data, wanted_images, my_shard, per_owner, pair_slots):
    owners, rank_hot = route_tables(wanted_images, per_owner, pair_slots)
    is_mine = (owners == my_shard).astype(jnp.float32)
    local_hot = (
        (wanted_images % per_owner)[:, :, None]
        == jnp.arange(per_owner, dtype=jnp.int32)[None, None, :]
    ).astype(jnp.float32)
    picker = jnp.einsum("scp,sci->spi", rank_hot * is_mine[:, :, None], local_hot).astype(
        jnp.bfloat16
    )
    return jnp.einsum("spi,if->spf", picker, row_data, preferred_element_type=jnp.float32).astype(
        jnp.bfloat16
    )


def unpack_rows(received, wanted_images, my_shard, per_owner, pair_slots):
    owners, rank_hot = route_tables(wanted_images, per_owner, pair_slots)
    owner_row = lax.dynamic_slice_in_dim(owners, my_shard, 1, 0)[0]
    rank_row = lax.dynamic_slice_in_dim(rank_hot, my_shard, 1, 0)[0]
    source_hot = (
        owner_row[:, None] == jnp.arange(received.shape[0], dtype=jnp.int32)[None, :]
    ).astype(jnp.float32)
    taker = (source_hot[:, :, None] * rank_row[:, None, :]).astype(jnp.bfloat16)
    return jnp.einsum("cop,opf->cf", taker, received, preferred_element_type=jnp.float32).astype(
        jnp.bfloat16
    )


def keyval_partial(flat_rows, cross_key, cross_value, head_cols, row_count):
    contract_first = (((0,), (1,)), ((), ()))
    block_count = row_count // (2 * head_cols)
    key_cols = lax.dot_general(
        cross_key, flat_rows, contract_first, preferred_element_type=jnp.float32
    )
    value_cols = lax.dot_general(
        cross_value, flat_rows, contract_first, preferred_element_type=jnp.float32
    )
    key_cols = key_cols.reshape(block_count, head_cols, flat_rows.shape[0])
    value_cols = value_cols.reshape(block_count, head_cols, flat_rows.shape[0])
    return jnp.concatenate([key_cols, value_cols], 1).reshape(row_count, flat_rows.shape[0])


def local(
    text_states,
    text_gain,
    gate_scale,
    live_counts,
    token_slot,
    wanted_images,
    patches,
    latent_init,
    context_gain,
    latent_gain,
    res_query,
    res_key,
    res_value,
    res_out,
    final_gain,
    cross_query,
    cross_key,
    cross_value,
    cross_out,
):
    my_feature = lax.axis_index("fsdp")
    my_shard = lax.axis_index("img")
    image_count = patches.shape[0]
    patch_count = patches.shape[1]
    feat_vis = patches.shape[2]
    latent_count = latent_init.shape[0]
    vis_width = latent_init.shape[1]
    res_cols = res_query.shape[1]
    res_heads = res_cols // RHD
    head_cols = cross_out.shape[0]
    token_count = text_states.shape[0]
    slot_count = wanted_images.shape[1]
    cross_heads = head_cols // HEAD
    contract_first = (((0,), (1,)), ((), ()))
    full_patches = lax.all_gather(patches, "fsdp", axis=2, tiled=True)
    context = layer_norm(full_patches, context_gain).astype(jnp.bfloat16)
    latent_normed = layer_norm(latent_init, latent_gain).astype(jnp.bfloat16)
    res_q_rows = jnp.dot(latent_normed, res_query, preferred_element_type=jnp.float32).astype(
        jnp.bfloat16
    )
    res_q_rows = res_q_rows.reshape(latent_count, res_heads, RHD)
    ctx_keys = jnp.einsum(
        "npv,vk->npk", context, res_key, preferred_element_type=jnp.float32
    ).astype(jnp.bfloat16)
    ctx_values = jnp.einsum(
        "npv,vk->npk", context, res_value, preferred_element_type=jnp.float32
    ).astype(jnp.bfloat16)
    lat_keys = jnp.dot(latent_normed, res_key, preferred_element_type=jnp.float32).astype(
        jnp.bfloat16
    )
    lat_values = jnp.dot(latent_normed, res_value, preferred_element_type=jnp.float32).astype(
        jnp.bfloat16
    )
    joined_shape = (image_count, latent_count, res_cols)
    key_rows = jnp.concatenate([ctx_keys, jnp.broadcast_to(lat_keys[None], joined_shape)], 1)
    value_rows = jnp.concatenate([ctx_values, jnp.broadcast_to(lat_values[None], joined_shape)], 1)
    key_rows = key_rows.reshape(image_count, patch_count + latent_count, res_heads, RHD)
    value_rows = value_rows.reshape(image_count, patch_count + latent_count, res_heads, RHD)
    res_scores = jnp.einsum(
        "rhe,nkhe->nhrk", res_q_rows, key_rows, preferred_element_type=jnp.float32
    ) * RHD ** (-0.5)
    res_weights = jnp.exp(res_scores)
    res_weights = (res_weights / jnp.sum(res_weights, -1, keepdims=True)).astype(jnp.bfloat16)
    res_mixed = jnp.einsum(
        "nhrk,nkhe->nrhe", res_weights, value_rows, preferred_element_type=jnp.float32
    )
    res_mixed = res_mixed.astype(jnp.bfloat16).reshape(image_count * latent_count, res_cols)
    columns = res_out
    mixed_sum = lax.psum_scatter(
        lax.dot_general(
            columns, res_mixed, contract_first, preferred_element_type=jnp.float32
        ).astype(jnp.bfloat16),
        "fsdp",
        scatter_dimension=0,
        tiled=True,
    ).astype(jnp.float32)
    init_cols = lax.dynamic_slice_in_dim(latent_init, my_feature * feat_vis, feat_vis, 1).astype(
        jnp.float32
    )
    latents = init_cols[None] + jnp.transpose(mixed_sum).reshape(
        image_count, latent_count, feat_vis
    )
    sum_first, sum_second = lax.psum((jnp.sum(latents, -1), jnp.sum(latents * latents, -1)), "fsdp")
    row_mean = sum_first / vis_width
    spread = sum_second / vis_width - row_mean * row_mean
    resampled = (
        (latents - row_mean[..., None]) * lax.rsqrt(spread + eps_norm)[..., None] * final_gain
    ).astype(jnp.bfloat16)
    text_f = text_states.astype(jnp.float32)
    squares = lax.psum(jnp.sum(text_f * text_f, -1), "fsdp")
    normed = (text_f * lax.rsqrt(squares / D + eps_rms)[:, None] * text_gain).astype(jnp.bfloat16)
    columns = cross_query
    query_cols = lax.psum_scatter(
        lax.dot_general(columns, normed, contract_first, preferred_element_type=jnp.float32).astype(
            jnp.bfloat16
        ),
        "fsdp",
        scatter_dimension=0,
        tiled=True,
    )
    per_image = resampled.reshape(image_count, latent_count * feat_vis)
    outgoing = pack_rows(per_image, wanted_images, my_shard, image_count, PAIR)
    incoming = lax.all_to_all(outgoing, "img", split_axis=0, concat_axis=0, tiled=True)
    slot_latents = unpack_rows(incoming, wanted_images, my_shard, image_count, PAIR).reshape(
        slot_count * latent_count, feat_vis
    )
    slot_kv = lax.psum_scatter(
        keyval_partial(
            slot_latents, cross_key, cross_value, head_cols, 2 * head_cols * lax.axis_size("fsdp")
        ).astype(jnp.bfloat16),
        "fsdp",
        scatter_dimension=0,
        tiled=True,
    )
    kv_slots = jnp.transpose(slot_kv.reshape(2 * head_cols, slot_count, latent_count), (1, 0, 2))
    query_heads = query_cols.reshape(cross_heads, HEAD, token_count)
    slot_keys = kv_slots[:, :head_cols].reshape(slot_count, cross_heads, HEAD, latent_count)
    slot_values = kv_slots[:, head_cols:].reshape(slot_count, cross_heads, HEAD, latent_count)
    scores = jnp.einsum(
        "het,cher->htcr", query_heads, slot_keys, preferred_element_type=jnp.float32
    ) * HEAD ** (-0.5)
    slot_hot = (token_slot[0][:, None] == jnp.arange(slot_count, dtype=jnp.int32)[None, :]).astype(
        jnp.float32
    )
    weights = jnp.exp(scores) * slot_hot[None, :, :, None]
    weights = (weights / jnp.sum(weights, axis=(2, 3), keepdims=True)).astype(jnp.bfloat16)
    attended = jnp.einsum(
        "htcr,cher->het", weights, slot_values, preferred_element_type=jnp.float32
    )
    attended = attended.astype(jnp.bfloat16).reshape(head_cols, token_count)
    columns = cross_out
    projected_cols = lax.psum_scatter(
        lax.dot_general(
            columns, attended, (((0,), (0,)), ((), ())), preferred_element_type=jnp.float32
        ).astype(jnp.bfloat16),
        "fsdp",
        scatter_dimension=0,
        tiled=True,
    ).astype(jnp.float32)
    projected = jnp.transpose(projected_cols)
    positions = jnp.arange(token_count, dtype=jnp.int32)
    live_mask = (positions < live_counts[0]).astype(jnp.float32)[:, None]
    return text_f + jnp.tanh(gate_scale) * projected * live_mask


def solution(mesh):
    placed = (
        P("img", "fsdp"),
        P("fsdp"),
        P("fsdp"),
        P("img"),
        P("img", None),
        P(),
        P("img", None, "fsdp"),
        P(),
        P(),
        P(),
        P(None, "fsdp"),
        P(None, "fsdp"),
        P(None, "fsdp"),
        P("fsdp", None),
        P("fsdp"),
        P("fsdp", None),
        P("fsdp", None),
        P("fsdp", None),
        P("fsdp", None),
    )
    return jax.shard_map(
        local, mesh=mesh, in_specs=placed, out_specs=P("img", "fsdp"), check_vma=False
    )
```

profile of v0, /device:TPU:0, one launch (start us, length us, event | category | flops | bytes accessed | tf_op | source)
XLA Modules:
  0.0 494.0 jit_solution(16812852713913608499)
XLA Ops:
  6.6 0.7 all-gather.2.cloned.1.call-update
  7.3 1.1 convert_reduce_fusion.1
  8.4 1.3 convolution_convert_fusion.10
  9.8 1.3 convolution_convert_fusion.11
  11.3 46.9 %all-gather.2.cloned.1.call-done = bf16[4,256,1280]{1,2,0:T(8,128)(2,1)} async-done(((bf16[4,256,80]{1,2,0:T(8,128)(2,1)}), bf16[4,256,1280]{1,2,0:T(8,128)(2,1)}) %all-gather.2.cloned.1.call-update) | async-done | bytes 2621456 | tf_op jit(solution)/shard_map/all_gather | solution.py:112
  58.2 2.4 convert_reduce_fusion
  60.6 2.8 convolution_convert_fusion.6
  64.2 2.8 convolution_convert_fusion.7
  67.7 1.1 copy.49
  69.1 72.8 %reduce-scatter.13.cloned.1.call-done = bf16[80,256]{1,0:T(8,128)(2,1)} async-done(((bf16[1280,256]{1,0:T(8,128)(2,1)}), bf16[80,256]{1,0:T(8,128)(2,1)}) %reduce-scatter.13.cloned.1.call-update) | async-done | bytes 40976
  141.9 0.9 copy.50
  143.1 38.6 %all-reduce = (f32[512]{0:T(512)S(1)}, f32[4,64]{1,0:T(4,128)S(1)}, f32[4,64]{1,0:T(4,128)S(1)}) all-reduce(f32[512]{0:T(512)S(1)} %fusion.15, f32[4,64]{1,0:T(4,128)S(1)} %reduce_sum.107, f32[4,64]{1,0:T(4,128)S(1)} %reduce_sum.105), channel_id=1, replica_groups=mesh['img'=8,'fsdp'=16] {'fsdp'}, use_global_device_ids=true, to_apply=%region_13.14 | all-reduce | flops 1024 | bytes 8192 | tf_op jit(solution)/shard_map/psum | solution.py:167
  181.7 10.2 %fusion = bf16[8192,512]{0,1:T(8,128)(2,1)} fusion(bf16[512,8192]{1,0:T(8,128)(2,1)} %param.34, bf16[512,512]{1,0:T(8,128)(2,1)S(1)} %copy-done.2, f32[512]{0:T(512)S(1)} %copy-done.14, f32[512]{0:T(512)S(1)} %add_rsqrt_fusion.1), kind=kOutput, calls=%fused_computation.5 | convolution fusion | flops 4300210176 | bytes 17305600 | tf_op jit(solution)/shard_map/dot_general | solution.py:171
  194.0 0.8 copy.39
  194.9 4.3 all-to-all-start
  199.5 6.2 %all-to-all-done = bf16[8,2,5120]{2,1,0:T(2,128)(2,1)S(1)} async-done(((bf16[8,2,5120]{2,1,0:T(2,128)(2,1)}), bf16[8,2,5120]{2,1,0:T(2,128)(2,1)S(1)}, u32[]{:S(2)}, u32[]{:S(2)}) %all-to-all-start) | async-done | bytes 163872 | tf_op jit(solution)/shard_map/all_to_all | solution.py:180
  206.1 5.6 %convolution_convert_fusion.3 = bf16[512,8192]{1,0:T(8,128)(2,1)} fusion(bf16[512,80]{1,0:T(8,128)(2,1)S(1)} %reshape.194, bf16[80,8192]{1,0:T(8,128)(2,1)S(1)} %copy-done), kind=kOutput, calls=%fused_computation.4 | convolution fusion | flops 675282944 | bytes 9781248 | tf_op jit(solution)/shard_map/dot_general | solution.py:66
  211.7 11.6 %copy.53 = bf16[64,8,16,512]{3,2,1,0:T(8,128)(2,1)} copy(bf16[64,8,16,512]{3,1,2,0:T(8,128)(2,1)} %bitcast.115) | data formatting | bytes 16777216
  223.2 5.5 %convolution_convert_fusion.2 = bf16[512,8192]{1,0:T(8,128)(2,1)} fusion(bf16[512,80]{1,0:T(8,128)(2,1)S(1)} %reshape.194, bf16[80,8192]{1,0:T(8,128)(2,1)S(1)} %copy-done.3), kind=kOutput, calls=%fused_computation.3 | convolution fusion | flops 675282944 | bytes 9781248 | tf_op jit(solution)/shard_map/dot_general | solution.py:69
  228.8 11.4 %copy.54 = bf16[64,8,16,512]{3,2,1,0:T(8,128)(2,1)} copy(bf16[64,8,16,512]{3,1,2,0:T(8,128)(2,1)} %bitcast.114) | data formatting | bytes 16777216
  240.2 8.4 %pad_maximum_fusion = bf16[16,1024,512]{1,0,2:T(8,128)(2,1)S(1)} fusion(bf16[16,512,512]{1,0,2:T(8,128)(2,1)} %bitcast.117, bf16[16,512,512]{1,0,2:T(8,128)(2,1)} %bitcast.116), kind=kLoop, calls=%fused_computation | loop fusion | flops 33554432 | bytes 33554432 | tf_op jit(solution)/shard_map/concatenate | solution.py:74
  248.6 12.0 %copy.55 = bf16[64,8,16,1024]{3,1,2,0:T(8,128)(2,1)} copy(bf16[64,8,16,1024]{3,2,1,0:T(8,128)(2,1)S(1)} %bitcast.113) | data formatting | bytes 33554432
  261.3 13.3 %reduce-scatter.9.cloned.1.call-done = bf16[512,512]{0,1:T(8,128)(2,1)} async-done(((bf16[8192,512]{0,1:T(8,128)(2,1)}), bf16[512,512]{0,1:T(8,128)(2,1)}) %reduce-scatter.9.cloned.1.call-update) | async-done | bytes 524304 | tf_op jit(solution)/shard_map/reduce_scatter | solution.py:170
  274.5 1.3 copy.48
  275.8 112.3 %reduce-scatter.7.cloned.1.call-done = bf16[1024,512]{0,1:T(8,128)(2,1)} async-done(((bf16[16384,512]{0,1:T(8,128)(2,1)}), bf16[1024,512]{0,1:T(8,128)(2,1)}) %reduce-scatter.7.cloned.1.call-update) | async-done | bytes 1048592 | tf_op jit(solution)/shard_map/reduce_scatter | solution.py:184
  388.1 1.3 slice_bitcast_fusion.1
  389.4 0.9 fusion.7
  390.3 1.0 fusion.11
  391.6 1.5 slice-done.1
  393.1 6.9 %fusion.1 = bf16[8192,512]{0,1:T(8,128)(2,1)} fusion(bf16[512,512]{1,0:T(8,128)(2,1)S(1)} %bitcast.122, bf16[512,8192]{1,0:T(8,128)(2,1)S(1)} %bitcast.119), kind=kOutput, calls=%fused_computation.6 | convolution fusion | flops 4299161600 | bytes 17301504 | tf_op jit(solution)/shard_map/dot_general | solution.py:210
  400.8 84.4 %reduce-scatter.11.cloned.1.call-done = bf16[512,512]{0,1:T(8,128)(2,1)} async-done(((bf16[8192,512]{0,1:T(8,128)(2,1)}), bf16[512,512]{0,1:T(8,128)(2,1)}) %reduce-scatter.11.cloned.1.call-update) | async-done | bytes 524304 | tf_op jit(solution)/shard_map/reduce_scatter | solution.py:209
  485.3 2.2 convert_add_fusion
  (83 shorter events, 6.0 us)
Async XLA Ops:
  6.5 199.6 %copy-start = (bf16[80,8192]{1,0:T(8,128)(2,1)S(1)}, bf16[80,8192]{1,0:T(8,128)(2,1)}, u32[]{:S(2)}) copy-start(bf16[80,8192]{1,0:T(8,128)(2,1)} %param.35) | copy-start | bytes 3932164
  6.5 56.9 %copy-start.5 = (bf16[64,1280]{1,0:T(8,128)(2,1)S(1)}, bf16[64,1280]{1,0:T(8,128)(2,1)}, u32[]{:S(2)}) copy-start(bf16[64,1280]{1,0:T(8,128)(2,1)} %param.26) | copy-start | bytes 491524
  6.5 56.9 %copy-start.12 = (f32[1280]{0:T(1024)S(1)}, f32[1280]{0:T(1024)}, u32[]{:S(2)}) copy-start(f32[1280]{0:T(1024)} %param.28) | copy-start | bytes 15364
  6.5 56.9 %copy-start.10 = (bf16[1280,96]{0,1:T(8,128)(2,1)S(1)}, bf16[1280,96]{0,1:T(8,128)(2,1)}, u32[]{:S(2)}) copy-start(bf16[1280,96]{0,1:T(8,128)(2,1)} %param.29) | copy-start | bytes 737284
  6.5 51.6 %all-gather.2.cloned.1.call-start = ((), (), s32[]{:S(2)}) async-start(), calls=%async_computation.5 | async-start | bytes 2785280 | tf_op jit(solution)/shard_map/all_gather | solution.py:112
  7.3 134.6 %reduce-scatter.13.cloned.1.call-start = ((), (), s32[]{:S(2)}) async-start(), calls=%async_computation.9 | async-start | bytes 696320
  9.8 54.3 %copy-start.11 = (bf16[1280,96]{0,1:T(8,128)(2,1)S(1)}, bf16[1280,96]{0,1:T(8,128)(2,1)}, u32[]{:S(2)}) copy-start(bf16[1280,96]{0,1:T(8,128)(2,1)} %param.31) | copy-start | bytes 737284
  9.8 54.3 %copy-start.13 = (f32[1280]{0:T(1024)S(1)}, f32[1280]{0:T(1024)}, u32[]{:S(2)}) copy-start(f32[1280]{0:T(1024)} %param.27) | copy-start | bytes 15364
  63.4 3.9 copy-start.4
  64.1 4.8 copy-start.2
  64.1 117.5 %copy-start.14 = (f32[512]{0:T(512)S(1)}, f32[512]{0:T(512)}, u32[]{:S(2)}) copy-start(f32[512]{0:T(512)} %param.20) | copy-start | bytes 6148
  68.8 205.8 %reduce-scatter.9.cloned.1.call-start = ((), (), s32[]{:S(2)}) async-start(), calls=%async_computation.7 | async-start | bytes 8912896 | tf_op jit(solution)/shard_map/reduce_scatter | solution.py:170
  191.9 0.7 copy-start.9
  191.9 0.7 copy-start.6
  194.9 10.7 %all-to-all-start = ((bf16[8,2,5120]{2,1,0:T(2,128)(2,1)}), bf16[8,2,5120]{2,1,0:T(2,128)(2,1)S(1)}, u32[]{:S(2)}, u32[]{:S(2)}) async-start(bf16[8,2,5120]{2,1,0:T(2,128)(2,1)} %copy.39), calls=%async_computation | async-start | bytes 327680 | tf_op jit(solution)/shard_map/all_to_all | solution.py:180
  199.2 188.9 %reduce-scatter.7.cloned.1.call-start = ((), (), s32[]{:S(2)}) async-start(), calls=%async_computation.6 | async-start | bytes 17825792 | tf_op jit(solution)/shard_map/reduce_scatter | solution.py:184
  211.7 11.6 %copy-start.3 = (bf16[80,8192]{1,0:T(8,128)(2,1)S(1)}, bf16[80,8192]{1,0:T(8,128)(2,1)}, u32[]{:S(2)}) copy-start(bf16[80,8192]{1,0:T(8,128)(2,1)} %param.36) | copy-start | bytes 3932164
  260.6 0.7 copy-start.7
  260.6 224.7 %reduce-scatter.11.cloned.1.call-start = ((), (), s32[]{:S(2)}) async-start(), calls=%async_computation.8 | async-start | bytes 8912896 | tf_op jit(solution)/shard_map/reduce_scatter | solution.py:209
  389.4 2.2 slice-start
  390.3 2.8 slice-start.1
  400.0 0.8 copy-start.8
  400.0 87.5 %copy-start.1 = (bf16[80,8192]{1,0:T(8,128)(2,1)S(1)}, bf16[80,8192]{1,0:T(8,128)(2,1)}, u32[]{:S(2)}) copy-start(bf16[80,8192]{1,0:T(8,128)(2,1)} %param.35) | copy-start | bytes 3932164
Sparse Core Ops, SparseCore 0:
  9.5 48.6 all-gather.1
  68.9 72.9 reduce-scatter.12
  192.1 82.4 reduce-scatter.8
  277.8 110.2 reduce-scatter.6
  400.2 85.0 reduce-scatter.10
where the time goes:
time: 495 us; the launch traced here: 494 us
  waiting for transfers between devices  337 us (68%)
  local copies, waits for them, and re-layouts  44.7 us (9%)
  matrix products  40.3 us (8%)
  blocking collectives  38.6 us (8%)
  other arithmetic  14.9 us (3%)
  between operations  14.3 us (3%)
    reduce_scatter x1, waiting for transfers between devices, local(): lax.psum_scatter(keyval_partial(slot_latents, cross_key, cross_value, hea...  112 us
    reduce_scatter x1, waiting for transfers between devices, local(): lax.psum_scatter(lax.dot_general(columns, attended, (((0,), (0,)), ((), (...  84.4 us
    unnamed x6, waiting for transfers between devices  73.5 us
    all_gather x1, waiting for transfers between devices, local(): full_patches = lax.all_gather(patches, 'fsdp', axis=2, tiled=True)  46.9 us
    unnamed x40, local copies, waits for them, and re-layouts  41.2 us
    psum x1, blocking collectives, local(): squares = lax.psum(jnp.sum(text_f * text_f, -1), 'fsdp')  38.6 us
    reduce_scatter x1, waiting for transfers between devices, local(): lax.psum_scatter(lax.dot_general(columns, normed, contract_first, preferr...  13.3 us
    dot_general x1, matrix products, local(): lax.dot_general(columns, normed, contract_first, preferred_element_type=j...  10.2 us
  transfers between devices with their start and end apart: 6, of which 6 were waited for; matrix products, arithmetic and copies ran while one was open for 13% of the time, Pallas kernels for 0%

commit v1 on v0

--- a/solution.py
+++ b/solution.py
@@ -164,7 +164,7 @@
         (latents - row_mean[..., None]) * lax.rsqrt(spread + eps_norm)[..., None] * final_gain
     ).astype(jnp.bfloat16)
     text_f = text_states.astype(jnp.float32)
-    squares = lax.psum(jnp.sum(text_f * text_f, -1), "fsdp")
+    squares = jnp.sum(lax.all_gather(jnp.sum(text_f * text_f, -1), "fsdp"), axis=0)
     normed = (text_f * lax.rsqrt(squares / D + eps_rms)[:, None] * text_gain).astype(jnp.bfloat16)
     columns = cross_query
     query_cols = lax.psum_scatter(

time: 495 us -> 461 us (0.931)
  waiting for transfers between devices: 337 us -> 277 us
  blocking collectives: 38.6 us -> 63.2 us
    all_gather x1, waiting for transfers between devices: 46.9 us -> 20.7 us  [local(): full_patches = lax.all_gather(patches, 'fsdp', axis=2, tiled=True)]
    all_gather x0 -> x1, blocking collectives: none -> 24.8 us  [local(): lax.all_gather(jnp.sum(text_f * text_f, -1), 'fsdp')]
    reduce_scatter x1, waiting for transfers between devices: 13.3 us -> 0.01 us  [local(): lax.psum_scatter(lax.dot_general(columns, normed, contract_first, preferr...]
    unnamed x6, waiting for transfers between devices: 73.5 us -> 62.3 us
    reduce_scatter x1, waiting for transfers between devices: 112 us -> 104 us  [local(): lax.psum_scatter(keyval_partial(slot_latents, cross_key, cross_value, hea...]
  transfers between devices with their start and end apart: 6 -> 6, of which waited for: 6 -> 5; matrix products, arithmetic and copies ran while one was open for 13% -> 16% of each run, Pallas kernels for 0% -> 0%
where the time goes in v1:
time: 461 us; the launch traced here: 460 us
  waiting for transfers between devices  277 us (60%)
  blocking collectives  63.2 us (14%)
  local copies, waits for them, and re-layouts  44.2 us (10%)
  matrix products  40.3 us (9%)
  other arithmetic  16.1 us (3%)
  between operations  14.3 us (3%)
  starting transfers between devices  4.73 us (1%)
    reduce_scatter x1, waiting for transfers between devices, local(): lax.psum_scatter(keyval_partial(slot_latents, cross_key, cross_value, hea...  104 us
    reduce_scatter x1, waiting for transfers between devices, local(): lax.psum_scatter(lax.dot_general(columns, attended, (((0,), (0,)), ((), (...  84.6 us
    unnamed x6, waiting for transfers between devices  62.3 us
    unnamed x40, local copies, waits for them, and re-layouts  40.7 us
    psum x1, blocking collectives, local(): lax.psum((jnp.sum(latents, -1), jnp.sum(latents * latents, -1)), 'fsdp')  38.4 us
    all_gather x1, blocking collectives, local(): lax.all_gather(jnp.sum(text_f * text_f, -1), 'fsdp')  24.8 us
    all_gather x1, waiting for transfers between devices, local(): full_patches = lax.all_gather(patches, 'fsdp', axis=2, tiled=True)  20.7 us
    dot_general x1, matrix products, local(): lax.dot_general(columns, normed, contract_first, preferred_element_type=j...  10.2 us
  transfers between devices with their start and end apart: 6, of which 5 were waited for; matrix products, arithmetic and copies ran while one was open for 16% of the time, Pallas kernels for 0%

profile of v1, /device:TPU:0, one launch (start us, length us, event | category | flops | bytes accessed | tf_op | source)
XLA Modules:
  0.0 460.2 jit_solution(15139078959241947730)
XLA Ops:
  7.3 1.1 convert_reduce_fusion.1
  8.4 1.4 convolution_convert_fusion.10
  9.9 1.3 convolution_convert_fusion.11
  11.3 1.3 fusion.15
  12.6 24.8 %all-gather.1 = f32[16,1,512]{2,1,0:T(1,128)S(1)} all-gather(f32[1,1,512]{2,1,0:T(1,128)S(1)} %bitcast.125), channel_id=2, replica_groups=mesh['img'=8,'fsdp'=16] {'fsdp'}, dimensions={0}, use_global_device_ids=true | all-gather | bytes 34816 | tf_op jit(solution)/shard_map/all_gather | solution.py:167
  37.5 20.7 %all-gather.4.cloned.1.call-done = bf16[4,256,1280]{1,2,0:T(8,128)(2,1)} async-done(((bf16[4,256,80]{1,2,0:T(8,128)(2,1)}), bf16[4,256,1280]{1,2,0:T(8,128)(2,1)}) %all-gather.4.cloned.1.call-update) | async-done | bytes 2621456 | tf_op jit(solution)/shard_map/all_gather | solution.py:112
  58.2 2.4 convert_reduce_fusion
  60.6 2.8 convolution_convert_fusion.6
  64.2 2.8 convolution_convert_fusion.7
  67.7 1.1 copy.49
  68.8 10.2 %fusion = bf16[8192,512]{0,1:T(8,128)(2,1)} fusion(bf16[512,8192]{1,0:T(8,128)(2,1)} %param.34, bf16[512,512]{1,0:T(8,128)(2,1)S(1)} %copy-done.2, f32[512]{0:T(512)S(1)} %copy-done.14, f32[512]{0:T(512)S(1)} %add_rsqrt_fusion.1), kind=kOutput, calls=%fused_computation.5 | convolution fusion | flops 4300210176 | bytes 17305600 | tf_op jit(solution)/shard_map/dot_general | solution.py:171
  80.3 61.5 %reduce-scatter.13.cloned.1.call-done = bf16[80,256]{1,0:T(8,128)(2,1)} async-done(((bf16[1280,256]{1,0:T(8,128)(2,1)}), bf16[80,256]{1,0:T(8,128)(2,1)}) %reduce-scatter.13.cloned.1.call-update) | async-done | bytes 40976
  141.8 0.9 copy.50
  143.1 38.4 %all-reduce = (f32[4,64]{1,0:T(4,128)S(1)}, f32[4,64]{1,0:T(4,128)S(1)}) all-reduce(f32[4,64]{1,0:T(4,128)S(1)} %reduce_sum.116, f32[4,64]{1,0:T(4,128)S(1)} %reduce_sum.114), channel_id=1, replica_groups=mesh['img'=8,'fsdp'=16] {'fsdp'}, use_global_device_ids=true, to_apply=%region_10.0 | all-reduce | flops 512 | bytes 4096 | tf_op jit(solution)/shard_map/psum | solution.py:160
  182.3 0.8 copy.39
  183.2 4.4 all-to-all-start
  187.9 6.2 %all-to-all-done = bf16[8,2,5120]{2,1,0:T(2,128)(2,1)S(1)} async-done(((bf16[8,2,5120]{2,1,0:T(2,128)(2,1)}), bf16[8,2,5120]{2,1,0:T(2,128)(2,1)S(1)}, u32[]{:S(2)}, u32[]{:S(2)}) %all-to-all-start) | async-done | bytes 163872 | tf_op jit(solution)/shard_map/all_to_all | solution.py:180
  194.5 5.5 %convolution_convert_fusion.3 = bf16[512,8192]{1,0:T(8,128)(2,1)} fusion(bf16[512,80]{1,0:T(8,128)(2,1)S(1)} %reshape.198, bf16[80,8192]{1,0:T(8,128)(2,1)S(1)} %copy-done), kind=kOutput, calls=%fused_computation.4 | convolution fusion | flops 675282944 | bytes 9781248 | tf_op jit(solution)/shard_map/dot_general | solution.py:66
  200.0 11.3 %copy.53 = bf16[64,8,16,512]{3,2,1,0:T(8,128)(2,1)} copy(bf16[64,8,16,512]{3,1,2,0:T(8,128)(2,1)} %bitcast.116) | data formatting | bytes 16777216
  211.3 5.5 %convolution_convert_fusion.2 = bf16[512,8192]{1,0:T(8,128)(2,1)} fusion(bf16[512,80]{1,0:T(8,128)(2,1)S(1)} %reshape.198, bf16[80,8192]{1,0:T(8,128)(2,1)S(1)} %copy-done.3), kind=kOutput, calls=%fused_computation.3 | convolution fusion | flops 675282944 | bytes 9781248 | tf_op jit(solution)/shard_map/dot_general | solution.py:69
  216.9 11.2 %copy.54 = bf16[64,8,16,512]{3,2,1,0:T(8,128)(2,1)} copy(bf16[64,8,16,512]{3,1,2,0:T(8,128)(2,1)} %bitcast.115) | data formatting | bytes 16777216
  228.1 8.4 %pad_maximum_fusion = bf16[16,1024,512]{1,0,2:T(8,128)(2,1)S(1)} fusion(bf16[16,512,512]{1,0,2:T(8,128)(2,1)} %bitcast.118, bf16[16,512,512]{1,0,2:T(8,128)(2,1)} %bitcast.117), kind=kLoop, calls=%fused_computation | loop fusion | flops 33554432 | bytes 33554432 | tf_op jit(solution)/shard_map/concatenate | solution.py:74
  236.4 12.1 %copy.55 = bf16[64,8,16,1024]{3,1,2,0:T(8,128)(2,1)} copy(bf16[64,8,16,1024]{3,2,1,0:T(8,128)(2,1)S(1)} %bitcast.114) | data formatting | bytes 33554432
  249.2 1.3 copy.48
  250.5 103.6 %reduce-scatter.7.cloned.1.call-done = bf16[1024,512]{0,1:T(8,128)(2,1)} async-done(((bf16[16384,512]{0,1:T(8,128)(2,1)}), bf16[1024,512]{0,1:T(8,128)(2,1)}) %reduce-scatter.7.cloned.1.call-update) | async-done | bytes 1048592 | tf_op jit(solution)/shard_map/reduce_scatter | solution.py:184
  354.1 1.3 slice_bitcast_fusion.1
  355.4 0.9 fusion.7
  356.3 1.0 fusion.11
  357.6 1.5 slice-done.1
  359.1 7.0 %fusion.1 = bf16[8192,512]{0,1:T(8,128)(2,1)} fusion(bf16[512,512]{1,0:T(8,128)(2,1)S(1)} %bitcast.123, bf16[512,8192]{1,0:T(8,128)(2,1)S(1)} %bitcast.120), kind=kOutput, calls=%fused_computation.6 | convolution fusion | flops 4299161600 | bytes 17301504 | tf_op jit(solution)/shard_map/dot_general | solution.py:210
  366.9 84.6 %reduce-scatter.11.cloned.1.call-done = bf16[512,512]{0,1:T(8,128)(2,1)} async-done(((bf16[8192,512]{0,1:T(8,128)(2,1)}), bf16[512,512]{0,1:T(8,128)(2,1)}) %reduce-scatter.11.cloned.1.call-update) | async-done | bytes 524304 | tf_op jit(solution)/shard_map/reduce_scatter | solution.py:209
  451.5 2.2 convert_add_fusion
  (85 shorter events, 6.5 us)
Async XLA Ops:
  6.5 188.0 %copy-start = (bf16[80,8192]{1,0:T(8,128)(2,1)S(1)}, bf16[80,8192]{1,0:T(8,128)(2,1)}, u32[]{:S(2)}) copy-start(bf16[80,8192]{1,0:T(8,128)(2,1)} %param.35) | copy-start | bytes 3932164
  6.5 51.7 %all-gather.4.cloned.1.call-start = ((), (), s32[]{:S(2)}) async-start(), calls=%async_computation.5 | async-start | bytes 2785280 | tf_op jit(solution)/shard_map/all_gather | solution.py:112
  7.3 134.6 %reduce-scatter.13.cloned.1.call-start = ((), (), s32[]{:S(2)}) async-start(), calls=%async_computation.9 | async-start | bytes 696320
  8.4 55.1 %copy-start.5 = (bf16[64,1280]{1,0:T(8,128)(2,1)S(1)}, bf16[64,1280]{1,0:T(8,128)(2,1)}, u32[]{:S(2)}) copy-start(bf16[64,1280]{1,0:T(8,128)(2,1)} %param.26) | copy-start | bytes 491524
  8.4 55.1 %copy-start.10 = (bf16[1280,96]{0,1:T(8,128)(2,1)S(1)}, bf16[1280,96]{0,1:T(8,128)(2,1)}, u32[]{:S(2)}) copy-start(bf16[1280,96]{0,1:T(8,128)(2,1)} %param.29) | copy-start | bytes 737284
  8.4 55.1 %copy-start.12 = (f32[1280]{0:T(1024)S(1)}, f32[1280]{0:T(1024)}, u32[]{:S(2)}) copy-start(f32[1280]{0:T(1024)} %param.28) | copy-start | bytes 15364
  11.3 52.8 %copy-start.11 = (bf16[1280,96]{0,1:T(8,128)(2,1)S(1)}, bf16[1280,96]{0,1:T(8,128)(2,1)}, u32[]{:S(2)}) copy-start(bf16[1280,96]{0,1:T(8,128)(2,1)} %param.31) | copy-start | bytes 737284
  11.3 52.8 %copy-start.13 = (f32[1280]{0:T(1024)S(1)}, f32[1280]{0:T(1024)}, u32[]{:S(2)}) copy-start(f32[1280]{0:T(1024)} %param.27) | copy-start | bytes 15364
  63.4 3.9 copy-start.4
  64.1 4.7 %copy-start.2 = (bf16[512,512]{1,0:T(8,128)(2,1)S(1)}, bf16[512,512]{1,0:T(8,128)(2,1)}, u32[]{:S(2)}) copy-start(bf16[512,512]{1,0:T(8,128)(2,1)} %param.19) | copy-start | bytes 1572868
  64.1 4.7 %copy-start.14 = (f32[512]{0:T(512)S(1)}, f32[512]{0:T(512)}, u32[]{:S(2)}) copy-start(f32[512]{0:T(512)} %param.20) | copy-start | bytes 6148
  68.8 180.4 %reduce-scatter.9.cloned.1.call-start = ((), (), s32[]{:S(2)}) async-start(), calls=%async_computation.7 | async-start | bytes 8912896 | tf_op jit(solution)/shard_map/reduce_scatter | solution.py:170
  79.1 0.7 copy-start.9
  79.1 0.7 copy-start.6
  183.2 10.8 %all-to-all-start = ((bf16[8,2,5120]{2,1,0:T(2,128)(2,1)}), bf16[8,2,5120]{2,1,0:T(2,128)(2,1)S(1)}, u32[]{:S(2)}, u32[]{:S(2)}) async-start(bf16[8,2,5120]{2,1,0:T(2,128)(2,1)} %copy.39), calls=%async_computation | async-start | bytes 327680 | tf_op jit(solution)/shard_map/all_to_all | solution.py:180
  187.6 166.5 %reduce-scatter.7.cloned.1.call-start = ((), (), s32[]{:S(2)}) async-start(), calls=%async_computation.6 | async-start | bytes 17825792 | tf_op jit(solution)/shard_map/reduce_scatter | solution.py:184
  200.0 11.3 %copy-start.3 = (bf16[80,8192]{1,0:T(8,128)(2,1)S(1)}, bf16[80,8192]{1,0:T(8,128)(2,1)}, u32[]{:S(2)}) copy-start(bf16[80,8192]{1,0:T(8,128)(2,1)} %param.36) | copy-start | bytes 3932164
  248.5 0.7 copy-start.7
  248.5 202.9 %reduce-scatter.11.cloned.1.call-start = ((), (), s32[]{:S(2)}) async-start(), calls=%async_computation.8 | async-start | bytes 8912896 | tf_op jit(solution)/shard_map/reduce_scatter | solution.py:209
  355.4 2.2 slice-start
  356.3 2.8 slice-start.1
  366.1 0.8 copy-start.8
  366.1 87.6 %copy-start.1 = (bf16[80,8192]{1,0:T(8,128)(2,1)S(1)}, bf16[80,8192]{1,0:T(8,128)(2,1)}, u32[]{:S(2)}) copy-start(bf16[80,8192]{1,0:T(8,128)(2,1)} %param.35) | copy-start | bytes 3932164
Sparse Core Ops, SparseCore 0:
  9.5 48.6 all-gather.3
  68.9 72.8 reduce-scatter.12
  145.3 85.2 reduce-scatter.8
  248.7 105.3 reduce-scatter.6
  366.2 85.1 reduce-scatter.10
